TPU v7x, 512 devices: a whole 4x8x8 slice. The times are simulated.
512 devices in a mesh: feat: 16 (over x, z_hi, core), samp: 32 (over y, z_lo).
Axes of the slice: x: 4, y: 8, z: 8 (z_hi: 2, z_lo: 4; z = z_hi * 4 + z_lo), core: 2. Of those that a mesh axis runs over, the one named last changes fastest.
Arguments:
- tier_one: bfloat16 [8192, 12288], P('feat', 'samp')
- residuals: bfloat16 [12288, 128], P('samp'), may hold values from -6 to 6
- pair_list: int32 [3, 65536], P(None, 'feat'), may hold values from 0 to 8191, as said below
Outputs:
- scores: float32 [65536, 128], P(('feat', 'samp'))
Inputs may be any that keep to these rules, and one draw needn't show every extreme that they name: `pair_list`: rows 0 and 1 are feature indices, row 2 an operator id of 0 to 3; each descriptor's two features differ.
All inputs are finite; a program needn't handle non-finite values.
Results may differ from a plain program's by a relative error of at most 0.0031.
Values may be sent and summed in bfloat16 or wider, within the bound.
No kernel may reach another device: no remote copies, remote signals or barrier semaphores. Data moves between devices by JAX's collectives and lax.ppermute only.
A program may use at most 64 MiB of HBM per device.

v0:
```python
import math
import jax
import jax.numpy as jnp
from jax import lax
from jax.sharding import PartitionSpec as P

epsilon = 1e-05


def combine_rows(first_rows, second_rows, operator_id):
    first_rows = first_rows.astype(jnp.float32)
    second_rows = second_rows.astype(jnp.float32)
    quotient = first_rows / (1.0 + jnp.abs(second_rows))
    built = jnp.where(
        operator_id == 0,
        first_rows + second_rows,
        jnp.where(
            operator_id == 1,
            first_rows - second_rows,
            jnp.where(operator_id == 2, first_rows * second_rows, quotient),
        ),
    )
    return built.astype(jnp.bfloat16)


def descriptors(tier_one, pair_cols):
    first_rows = jnp.take(tier_one, pair_cols[0], axis=0)
    second_rows = jnp.take(tier_one, pair_cols[1], axis=0)
    return combine_rows(first_rows, second_rows, pair_cols[2][:, None])


def project_block(built, residuals):
    product = jnp.dot(built, residuals, preferred_element_type=jnp.float32)
    widened = built.astype(jnp.float32)
    return (product, jnp.sum(widened, axis=1), jnp.sum(widened * widened, axis=1))


def block_terms(tier_one, residuals, pair_cols):
    return project_block(descriptors(tier_one, pair_cols), residuals)


def finish(product, first_sums, square_sums, col_totals, sample_count):
    means = first_sums / sample_count
    variance = square_sums / sample_count - means * means
    centred = product - means[:, None] * col_totals[None, :]
    return centred * lax.rsqrt(variance + epsilon)[:, None] / math.sqrt(sample_count)


def per_device(tier_one, residuals, pair_list):
    local_pairs = pair_list.shape[1]
    width_k = residuals.shape[1]
    block_size = math.gcd(local_pairs, 1024)
    block_count = local_pairs // block_size
    grouped = pair_list.reshape(3, block_count, block_size).transpose(1, 0, 2)
    whole_rows = lax.all_gather(tier_one, "feat", axis=0, tiled=True)
    product, first_sums, square_sums = lax.map(
        lambda pair_cols: block_terms(whole_rows, residuals, pair_cols), grouped
    )
    product = product.reshape(local_pairs, width_k)
    first_sums = first_sums.reshape(local_pairs)
    square_sums = square_sums.reshape(local_pairs)
    col_totals = jnp.sum(residuals.astype(jnp.float32), axis=0)
    sample_count = residuals.shape[0] * lax.axis_size("samp")
    first_sums, square_sums, col_totals = lax.psum((first_sums, square_sums, col_totals), "samp")
    owned = lax.psum_scatter(product, "samp", scatter_dimension=0, tiled=True)
    owned_rows = owned.shape[0]
    row_start = lax.axis_index("samp") * owned_rows
    first_sums = lax.dynamic_slice_in_dim(first_sums, row_start, owned_rows, 0)
    square_sums = lax.dynamic_slice_in_dim(square_sums, row_start, owned_rows, 0)
    return finish(owned, first_sums, square_sums, col_totals, sample_count)


def solution(mesh):
    in_specs = (P("feat", "samp"), P("samp", None), P(None, "feat"))
    out_specs = P(("feat", "samp"), None)
    return jax.shard_map(
        per_device, mesh=mesh, in_specs=in_specs, out_specs=out_specs, check_vma=False
    )
```

profile of v0, /device:TPU:6, one launch (start us, length us, event | category | flops | bytes accessed | tf_op | source)
XLA Modules:
  0.0 361.1 jit_solution(16862348691693398649)
XLA Ops:
  7.3 105.8 %all-gather.2.cloned.1.call-done = bf16[8192,384]{1,0:T(8,128)(2,1)} async-done(((bf16[512,384]{1,0:T(8,128)(2,1)}), bf16[8192,384]{1,0:T(8,128)(2,1)}) %all-gather.2.cloned.1.call-update) | async-done | bytes 6291472 | tf_op jit(solution)/shard_map/all_gather | solution.py:55
  113.1 78.5 %while.14 = (s32[]{:T(128)}, f32[4,1024,128]{2,1,0:T(8,128)}, f32[4,1024]{1,0:T(4,128)S(1)}, f32[4,1024]{1,0:T(4,128)S(1)}, s32[4,3,1024]{2,1,0:T(4,128)}, /*ind...) while((s32[]{:T(128)}, f32[4,1024,128]{2,1,0:T(8,128)}, ...), condition=%wide.region_3.5_spmd, body=%wide.region_0.4_spmd.sunk | while | flops 107762688 | bytes 7395525 | solution.py:56
  113.9 0.8 constant_dynamic-slice_fusion.4
  114.7 7.4 %gather_fusion = bf16[1024,384]{1,0:T(8,128)(2,1)S(1)} fusion(bf16[8192,384]{1,0:T(8,128)(2,1)} %get-tuple-element.169, s32[1024]{0:T(1024)S(1)} %fusion.20), kind=kCustom, calls=%fused_computation.1.clone.clone.1 | custom fusion | bytes 1576960 | tf_op jit(solution)/shard_map/while/body/eval_jaxpr/jit(_take)/gather | solution.py:28
  122.1 7.4 %gather_fusion.1 = bf16[1024,384]{1,0:T(8,128)(2,1)S(1)} fusion(bf16[8192,384]{1,0:T(8,128)(2,1)} %get-tuple-element.169, s32[1024]{0:T(1024)S(1)} %fusion.21), kind=kCustom, calls=%fused_computation.clone.clone.1 | custom fusion | bytes 1576960 | tf_op jit(solution)/shard_map/while/body/eval_jaxpr/jit(_take)/gather | solution.py:27
  129.5 1.9 fusion.22
  131.5 1.2 fusion.23
  133.5 0.8 constant_dynamic-slice_fusion.4
  134.3 7.4 %gather_fusion = bf16[1024,384]{1,0:T(8,128)(2,1)S(1)} fusion(bf16[8192,384]{1,0:T(8,128)(2,1)} %get-tuple-element.169, s32[1024]{0:T(1024)S(1)} %fusion.20), kind=kCustom, calls=%fused_computation.1.clone.clone.1 | custom fusion | bytes 1576960 | tf_op jit(solution)/shard_map/while/body/eval_jaxpr/jit(_take)/gather | solution.py:28
  141.7 7.4 %gather_fusion.1 = bf16[1024,384]{1,0:T(8,128)(2,1)S(1)} fusion(bf16[8192,384]{1,0:T(8,128)(2,1)} %get-tuple-element.169, s32[1024]{0:T(1024)S(1)} %fusion.21), kind=kCustom, calls=%fused_computation.clone.clone.1 | custom fusion | bytes 1576960 | tf_op jit(solution)/shard_map/while/body/eval_jaxpr/jit(_take)/gather | solution.py:27
  149.1 1.9 fusion.22
  151.1 1.2 fusion.23
  154.0 7.4 %gather_fusion = bf16[1024,384]{1,0:T(8,128)(2,1)S(1)} fusion(bf16[8192,384]{1,0:T(8,128)(2,1)} %get-tuple-element.169, s32[1024]{0:T(1024)S(1)} %fusion.20), kind=kCustom, calls=%fused_computation.1.clone.clone.1 | custom fusion | bytes 1576960 | tf_op jit(solution)/shard_map/while/body/eval_jaxpr/jit(_take)/gather | solution.py:28
  161.3 7.4 %gather_fusion.1 = bf16[1024,384]{1,0:T(8,128)(2,1)S(1)} fusion(bf16[8192,384]{1,0:T(8,128)(2,1)} %get-tuple-element.169, s32[1024]{0:T(1024)S(1)} %fusion.21), kind=kCustom, calls=%fused_computation.clone.clone.1 | custom fusion | bytes 1576960 | tf_op jit(solution)/shard_map/while/body/eval_jaxpr/jit(_take)/gather | solution.py:27
  168.7 1.9 fusion.22
  170.8 1.2 fusion.23
  173.5 7.4 %gather_fusion = bf16[1024,384]{1,0:T(8,128)(2,1)S(1)} fusion(bf16[8192,384]{1,0:T(8,128)(2,1)} %get-tuple-element.169, s32[1024]{0:T(1024)S(1)} %fusion.20), kind=kCustom, calls=%fused_computation.1.clone.clone.1 | custom fusion | bytes 1576960 | tf_op jit(solution)/shard_map/while/body/eval_jaxpr/jit(_take)/gather | solution.py:28
  180.9 7.4 %gather_fusion.1 = bf16[1024,384]{1,0:T(8,128)(2,1)S(1)} fusion(bf16[8192,384]{1,0:T(8,128)(2,1)} %get-tuple-element.169, s32[1024]{0:T(1024)S(1)} %fusion.21), kind=kCustom, calls=%fused_computation.clone.clone.1 | custom fusion | bytes 1576960 | tf_op jit(solution)/shard_map/while/body/eval_jaxpr/jit(_take)/gather | solution.py:27
  188.3 1.9 fusion.22
  190.4 1.2 fusion.23
  191.6 0.9 copy-done.1
  192.5 151.1 %all-reduce = (f32[4096]{0:T(1024)S(1)}, f32[4096]{0:T(1024)S(1)}, f32[128]{0:T(128)S(1)}) all-reduce(f32[4096]{0:T(1024)S(1)} %get-tuple-element.77, f32[4096]{0:T(1024)S(1)} %get-tuple-element.78, f32[128]{0:T(128)S(1)} %convert_reduce_fusion.1), channel_id=1, replica_groups=mesh['feat'=16,'samp'=32] {'samp'}, use_global_device_ids=true, to_apply=%region_8.10 | all-reduce | flops 8320 | bytes 66560 | tf_op jit(solution)/shard_map/psum | solution.py:64
  343.7 9.1 %reduce-scatter.2.cloned.1.call-done = f32[128,128]{1,0:T(8,128)} async-done(((f32[4096,128]{1,0:T(8,128)}), f32[128,128]{1,0:T(8,128)}) %reduce-scatter.2.cloned.1.call-update) | async-done | bytes 65552 | tf_op jit(solution)/shard_map/reduce_scatter | solution.py:65
  352.7 1.6 multiply_multiply_fusion
  (45 shorter events, 6.3 us)
Async XLA Ops:
  6.5 106.6 %all-gather.2.cloned.1.call-start = ((), (), s32[]{:S(2)}) async-start(), calls=%async_computation.1 | async-start | bytes 6684672 | tf_op jit(solution)/shard_map/all_gather | solution.py:55
  7.3 345.5 %reduce-scatter.2.cloned.1.call-start = ((), (), s32[]{:S(2)}) async-start(), calls=%async_computation.2 | async-start | bytes 2162688 | tf_op jit(solution)/shard_map/reduce_scatter | solution.py:65
  129.5 2.1 copy-start
  149.1 2.1 copy-start
  168.7 2.1 copy-start
  188.3 2.1 copy-start
  191.6 0.9 copy-start.1
Sparse Core Ops, SparseCore 0:
  10.6 102.4 all-gather.1
  191.7 160.9 reduce-scatter.1
where the time goes:
time: 362 us; the launch traced here: 361 us
  blocking collectives  151 us (42%)
  waiting for transfers between devices  116 us (32%)
  local copies, waits for them, and re-layouts  63.7 us (18%)
  between operations  13.4 us (4%)
  other arithmetic  12.4 us (3%)
  matrix products  4.72 us (1%)
    psum x1, blocking collectives, per_device(): lax.psum((first_sums, square_sums, col_totals), 'samp')  151 us
    all_gather x1, waiting for transfers between devices, per_device(): whole_rows = lax.all_gather(tier_one, 'feat', axis=0, tiled=True)  106 us
    gather x4, local copies, waits for them, and re-layouts, descriptors(): second_rows = jnp.take(tier_one, pair_cols[1], axis=0)  29.5 us
    gather x4, local copies, waits for them, and re-layouts, descriptors(): first_rows = jnp.take(tier_one, pair_cols[0], axis=0)  29.5 us
    reduce_scatter x1, waiting for transfers between devices, per_device(): owned = lax.psum_scatter(product, 'samp', scatter_dimension=0, tiled=True)  9.07 us
    reduce_sum x4, other arithmetic, project_block(): jnp.sum(widened * widened, axis=1)  7.52 us
  transfers between devices with their start and end apart: 2, of which 2 were waited for; matrix products, arithmetic and copies ran while one was open for 0% of the time, Pallas kernels for 0%

commit v1 on v0

--- a/solution.py
+++ b/solution.py
@@ -52,7 +52,9 @@
     block_size = math.gcd(local_pairs, 1024)
     block_count = local_pairs // block_size
     grouped = pair_list.reshape(3, block_count, block_size).transpose(1, 0, 2)
-    whole_rows = lax.all_gather(tier_one, "feat", axis=0, tiled=True)
+    whole_rows = jnp.concatenate(
+        lax.all_to_all(jnp.stack([tier_one] * lax.axis_size("feat")), "feat", 0, 0), axis=0
+    )
     product, first_sums, square_sums = lax.map(
         lambda pair_cols: block_terms(whole_rows, residuals, pair_cols), grouped
     )

time: 362 us -> 421 us (1.16)
  blocking collectives: 151 us -> 224 us
  waiting for transfers between devices: 116 us -> 84.7 us
  starting transfers between devices: 0.04 us -> 13.4 us
    all_gather x1 -> x0, waiting for transfers between devices: 106 us -> none  [per_device(): whole_rows = lax.all_gather(tier_one, 'feat', axis=0, tiled=True)]
    all_to_all x0 -> x1, waiting for transfers between devices: none -> 75.5 us  [per_device(): lax.all_to_all(jnp.stack([tier_one] * lax.axis_size('feat')), 'feat', 0, 0)]
    psum x1, blocking collectives: 151 us -> 224 us  [per_device(): lax.psum((first_sums, square_sums, col_totals), 'samp')]
    all_to_all x0 -> x1, starting transfers between devices: none -> 13.4 us  [per_device(): lax.all_to_all(jnp.stack([tier_one] * lax.axis_size('feat')), 'feat', 0, 0)]
    another operation x0 -> x1, local copies, waits for them, and re-layouts: none -> 4.46 us  [per_device(): jnp.stack([tier_one] * lax.axis_size('feat'))]
where the time goes in v1:
time: 421 us; the launch traced here: 420 us
  blocking collectives  224 us (53%)
  waiting for transfers between devices  84.7 us (20%)
  local copies, waits for them, and re-layouts  67.1 us (16%)
  starting transfers between devices  13.4 us (3%)
  between operations  13.4 us (3%)
  other arithmetic  12.4 us (3%)
  matrix products  4.75 us (1%)
    psum x1, blocking collectives, per_device(): lax.psum((first_sums, square_sums, col_totals), 'samp')  224 us
    all_to_all x1, waiting for transfers between devices, per_device(): lax.all_to_all(jnp.stack([tier_one] * lax.axis_size('feat')), 'feat', 0, 0)  75.5 us
    gather x4, local copies, waits for them, and re-layouts, descriptors(): second_rows = jnp.take(tier_one, pair_cols[1], axis=0)  29.5 us
    gather x4, local copies, waits for them, and re-layouts, descriptors(): first_rows = jnp.take(tier_one, pair_cols[0], axis=0)  29.5 us
    all_to_all x1, starting transfers between devices, per_device(): lax.all_to_all(jnp.stack([tier_one] * lax.axis_size('feat')), 'feat', 0, 0)  13.4 us
    reduce_scatter x1, waiting for transfers between devices, per_device(): owned = lax.psum_scatter(product, 'samp', scatter_dimension=0, tiled=True)  9.28 us
  transfers between devices with their start and end apart: 2, of which 2 were waited for; matrix products, arithmetic and copies ran while one was open for 0% of the time, Pallas kernels for 0%

profile of v1, /device:TPU:6, one launch (start us, length us, event | category | flops | bytes accessed | tf_op | source)
XLA Modules:
  0.0 419.8 jit_solution(9682175932418146393)
XLA Ops:
  6.5 4.5 %stack.2 = bf16[16,512,384]{2,1,0:T(8,128)(2,1)} broadcast(bf16[512,384]{1,0:T(8,128)(2,1)} %param.7), dimensions={1,2} | broadcast | bytes 6684672 | tf_op jit(solution)/shard_map/stack | solution.py:56
  11.0 13.4 %all-to-all-start = ((bf16[16,512,384]{2,1,0:T(8,128)(2,1)}), bf16[16,512,384]{2,1,0:T(8,128)(2,1)}, u32[]{:S(2)}, u32[]{:S(2)}) async-start(bf16[16,512,384]{2,1,0:T(8,128)(2,1)} %stack.2), calls=%async_computation | async-start | bytes 12582912 | tf_op jit(solution)/shard_map/all_to_all | solution.py:56
  24.4 75.5 %all-to-all-done = bf16[16,512,384]{2,1,0:T(8,128)(2,1)} async-done(((bf16[16,512,384]{2,1,0:T(8,128)(2,1)}), bf16[16,512,384]{2,1,0:T(8,128)(2,1)}, u32[]{:S(2)}, u32[]{:S(2)}) %all-to-all-start) | async-done | bytes 6291488 | tf_op jit(solution)/shard_map/all_to_all | solution.py:56
  99.9 78.4 %while.14 = (s32[]{:T(128)}, f32[4,1024,128]{2,1,0:T(8,128)}, f32[4,1024]{1,0:T(4,128)S(1)}, f32[4,1024]{1,0:T(4,128)S(1)}, s32[4,3,1024]{2,1,0:T(4,128)}, /*ind...) while((s32[]{:T(128)}, f32[4,1024,128]{2,1,0:T(8,128)}, ...), condition=%wide.region_3.5_spmd, body=%wide.region_0.4_spmd.sunk | while | flops 107762688 | bytes 7002781 | solution.py:58
  100.7 7.4 %gather_fusion = bf16[1024,384]{1,0:T(8,128)(2,1)S(1)} fusion(bf16[8192,384]{1,0:T(8,128)(2,1)} %get-tuple-element.169, s32[1024]{0:T(1024)S(1)} %fusion.20), kind=kCustom, calls=%fused_computation.1.clone.clone.1 | custom fusion | bytes 1576960 | tf_op jit(solution)/shard_map/while/body/eval_jaxpr/jit(_take)/gather | solution.py:28
  108.1 7.4 %gather_fusion.1 = bf16[1024,384]{1,0:T(8,128)(2,1)S(1)} fusion(bf16[8192,384]{1,0:T(8,128)(2,1)} %get-tuple-element.169, s32[1024]{0:T(1024)S(1)} %fusion.21), kind=kCustom, calls=%fused_computation.clone.clone.1 | custom fusion | bytes 1576960 | tf_op jit(solution)/shard_map/while/body/eval_jaxpr/jit(_take)/gather | solution.py:27
  116.3 1.9 fusion.22
  118.2 1.2 fusion.23
  120.3 7.4 %gather_fusion = bf16[1024,384]{1,0:T(8,128)(2,1)S(1)} fusion(bf16[8192,384]{1,0:T(8,128)(2,1)} %get-tuple-element.169, s32[1024]{0:T(1024)S(1)} %fusion.20), kind=kCustom, calls=%fused_computation.1.clone.clone.1 | custom fusion | bytes 1576960 | tf_op jit(solution)/shard_map/while/body/eval_jaxpr/jit(_take)/gather | solution.py:28
  127.7 7.4 %gather_fusion.1 = bf16[1024,384]{1,0:T(8,128)(2,1)S(1)} fusion(bf16[8192,384]{1,0:T(8,128)(2,1)} %get-tuple-element.169, s32[1024]{0:T(1024)S(1)} %fusion.21), kind=kCustom, calls=%fused_computation.clone.clone.1 | custom fusion | bytes 1576960 | tf_op jit(solution)/shard_map/while/body/eval_jaxpr/jit(_take)/gather | solution.py:27
  135.9 1.9 fusion.22
  137.8 1.2 fusion.23
  139.1 0.8 constant_dynamic-slice_fusion.4
  140.0 7.4 %gather_fusion = bf16[1024,384]{1,0:T(8,128)(2,1)S(1)} fusion(bf16[8192,384]{1,0:T(8,128)(2,1)} %get-tuple-element.169, s32[1024]{0:T(1024)S(1)} %fusion.20), kind=kCustom, calls=%fused_computation.1.clone.clone.1 | custom fusion | bytes 1576960 | tf_op jit(solution)/shard_map/while/body/eval_jaxpr/jit(_take)/gather | solution.py:28
  147.4 7.4 %gather_fusion.1 = bf16[1024,384]{1,0:T(8,128)(2,1)S(1)} fusion(bf16[8192,384]{1,0:T(8,128)(2,1)} %get-tuple-element.169, s32[1024]{0:T(1024)S(1)} %fusion.21), kind=kCustom, calls=%fused_computation.clone.clone.1 | custom fusion | bytes 1576960 | tf_op jit(solution)/shard_map/while/body/eval_jaxpr/jit(_take)/gather | solution.py:27
  155.5 1.9 fusion.22
  157.4 1.2 fusion.23
  159.6 7.4 %gather_fusion = bf16[1024,384]{1,0:T(8,128)(2,1)S(1)} fusion(bf16[8192,384]{1,0:T(8,128)(2,1)} %get-tuple-element.169, s32[1024]{0:T(1024)S(1)} %fusion.20), kind=kCustom, calls=%fused_computation.1.clone.clone.1 | custom fusion | bytes 1576960 | tf_op jit(solution)/shard_map/while/body/eval_jaxpr/jit(_take)/gather | solution.py:28
  166.9 7.4 %gather_fusion.1 = bf16[1024,384]{1,0:T(8,128)(2,1)S(1)} fusion(bf16[8192,384]{1,0:T(8,128)(2,1)} %get-tuple-element.169, s32[1024]{0:T(1024)S(1)} %fusion.21), kind=kCustom, calls=%fused_computation.clone.clone.1 | custom fusion | bytes 1576960 | tf_op jit(solution)/shard_map/while/body/eval_jaxpr/jit(_take)/gather | solution.py:27
  175.1 1.9 fusion.22
  177.0 1.2 fusion.23
  178.4 223.6 %all-reduce = (f32[4096]{0:T(1024)S(1)}, f32[4096]{0:T(1024)S(1)}, f32[128]{0:T(128)S(1)}) all-reduce(f32[4096]{0:T(1024)S(1)} %get-tuple-element.77, f32[4096]{0:T(1024)S(1)} %get-tuple-element.78, f32[128]{0:T(128)S(1)} %convert_reduce_fusion.1), channel_id=1, replica_groups=mesh['feat'=16,'samp'=32] {'samp'}, use_global_device_ids=true, to_apply=%region_8.10 | all-reduce | flops 8320 | bytes 66560 | tf_op jit(solution)/shard_map/psum | solution.py:66
  402.1 9.3 %reduce-scatter.2.cloned.1.call-done = f32[128,128]{1,0:T(8,128)} async-done(((f32[4096,128]{1,0:T(8,128)}), f32[128,128]{1,0:T(8,128)}) %reduce-scatter.2.cloned.1.call-update) | async-done | bytes 65552 | tf_op jit(solution)/shard_map/reduce_scatter | solution.py:67
  411.3 1.6 multiply_multiply_fusion
  (37 shorter events, 6.3 us)
Async XLA Ops:
  11.0 88.9 %copy-start = (bf16[384,128]{1,0:T(8,128)(2,1)S(1)}, bf16[384,128]{1,0:T(8,128)(2,1)}, u32[]{:S(2)}) copy-start(bf16[384,128]{1,0:T(8,128)(2,1)} %param.8) | copy-start | bytes 294916
  11.0 88.9 %all-to-all-start = ((bf16[16,512,384]{2,1,0:T(8,128)(2,1)}), bf16[16,512,384]{2,1,0:T(8,128)(2,1)}, u32[]{:S(2)}, u32[]{:S(2)}) async-start(bf16[16,512,384]{2,1,0:T(8,128)(2,1)} %stack.2), calls=%async_computation | async-start | bytes 12582912 | tf_op jit(solution)/shard_map/all_to_all | solution.py:56
  24.4 387.0 %reduce-scatter.2.cloned.1.call-start = ((), (), s32[]{:S(2)}) async-start(), calls=%async_computation.2 | async-start | bytes 2162688 | tf_op jit(solution)/shard_map/reduce_scatter | solution.py:67
Sparse Core Ops, SparseCore 0:
  178.4 232.8 reduce-scatter.1
